TPU v7x, 32 devices: a whole 2x2x4 slice. The times are simulated.
32 devices in a mesh: row: 8 (over z, core), col: 4 (over y, x).
Axes of the slice: x: 2, y: 2, z: 4, core: 2. Of those that a mesh axis runs over, the one named last changes fastest.
Arguments:
- demand: float32 [2048, 4096], P('row', 'col'), may hold values from 0.2 to 2
- leakage: float32 [2048, 4096], P('row', 'col'), may hold values from 0.05 to 0.5
- conductance: float32 [2048, 4096], P('row', 'col'), may hold values from 0.5 to 4
- vias: int32 [2048, 4096], P('row', 'col'), may hold values 0 or 1
- layer_of: int32 [256, 512], P('row'), may hold values from 0 to 31
- lateral_k: float32 [32, 256, 512], P('col', 'row'), may hold values from 0.3 to 3
- vertical_k: float32 [32, 256, 512], P('col', 'row'), may hold values from 0.1 to 1
Outputs:
- drop: float32 [2048, 4096], P('row', 'col')
- temperature: float32 [32, 256, 512], P('col', 'row')
All inputs are finite; a program needn't handle non-finite values. No bound on the sum of `vias` on one device may be relied on, other than what follows from the above.
Results may differ from a plain program's by a relative error of at most 0.0001.
Values sent between devices are 32-bit elements; how exact they have to be, the bound alone decides.
No kernel may reach another device: no remote copies, remote signals or barrier semaphores. Data moves between devices by JAX's collectives and lax.ppermute only.
A program may use at most 128 MiB of HBM per device.

v0:
```python
import functools
import os

import jax
import jax.numpy as jnp
from jax import lax
from jax.experimental import pallas as pl
from jax.experimental.pallas import tpu as pltpu
from jax.sharding import PartitionSpec as P

INTERPRET = os.environ.get("SOL_INTERPRET") == "1"
UNROLL = 8

COARSE = 8
SWEEPS = 4
HEAT_SWEEPS = 4
OUTER = 2


COND_SLOPE = 0.5
LEAK_SLOPE = 0.7
VIA_CONDUCT = 4.0

HALO = 4


def extended(block, sides):
    for axis, dim, width in sides:
        count = lax.axis_size(axis)
        forward = [(i, i + 1) for i in range(count - 1)]
        backward = [(target, source) for source, target in forward]
        low = lax.ppermute(
            lax.slice_in_dim(block, block.shape[dim] - width, None, axis=dim), axis, forward
        )
        high = lax.ppermute(lax.slice_in_dim(block, 0, width, axis=dim), axis, backward)
        block = jnp.concatenate([low, block, high], axis=dim)
    return block


def spread_cols(coarse, fine_cols):
    n = coarse.shape[1]
    ids = jnp.arange(fine_cols, dtype=jnp.int32) // COARSE
    onehot = (jnp.arange(n, dtype=jnp.int32)[:, None] == ids[None, :]).astype(jnp.float32)
    return jnp.dot(coarse, onehot, precision=lax.Precision.HIGHEST)


def fine_of(coarse, fine_cols):
    wide = spread_cols(coarse, fine_cols)
    rows = wide.shape[0]
    return jnp.broadcast_to(wide[:, None, :], (rows, COARSE, fine_cols)).reshape(rows * COARSE, fine_cols)


def coarse_of(fine):
    rows, cols = fine.shape
    summed_rows = jnp.sum(fine.reshape(rows // COARSE, COARSE, cols), axis=1)
    n = cols // COARSE
    ids = jnp.arange(cols, dtype=jnp.int32) // COARSE
    onehot = (ids[:, None] == jnp.arange(n, dtype=jnp.int32)[None, :]).astype(jnp.float32)
    return jnp.dot(summed_rows, onehot, precision=lax.Precision.HIGHEST) * (1.0 / (COARSE * COARSE))


def row_above(x, above):
    sub = lax.broadcasted_iota(jnp.int32, x.shape, 0)
    edge = jnp.broadcast_to(above[x.shape[0] - 1:, :], x.shape)
    return jnp.where(sub == 0, edge, pltpu.roll(x, 1, 0))


def row_below(x, below):
    n = x.shape[0]
    sub = lax.broadcasted_iota(jnp.int32, x.shape, 0)
    edge = jnp.broadcast_to(below[:1, :], x.shape)
    return jnp.where(sub == n - 1, edge, pltpu.roll(x, n - 1, 0))


def rows_of(k):
    return pl.ds(pl.multiple_of(k * 8, 8), 8)


def chunk(ref, k, count):
    return ref[rows_of(jnp.clip(k, 0, count - 1)), :]


def power_kernel(*refs, zero_start, stacked, offset):
    refs = list(refs)
    d_ref = None if zero_start else refs.pop(0)
    if stacked:
        p_ref = refs.pop(0)
        c_ref, l_ref, v_ref = p_ref.at[0], p_ref.at[1], p_ref.at[2]
    else:
        c_ref, l_ref, v_ref = refs.pop(0), refs.pop(0), refs.pop(0)
        v_ref = v_ref.at[2]
    rok_ref, cok_ref, o_ref, wn_ref, ws_ref, ww_ref, we_ref, inv_ref, buf_ref = refs
    n, w = o_ref.shape
    count = n // 8

    def weights(k, carry):
        sl = rows_of(k)
        x = c_ref[sl, :]
        a = (x + row_above(x, chunk(c_ref, k - 1, count))) * 0.5
        b = (x + row_below(x, chunk(c_ref, k + 1, count))) * 0.5
        e = (x + pltpu.roll(x, 1, 1)) * 0.5
        f = (x + pltpu.roll(x, w - 1, 1)) * 0.5
        wn_ref[sl, :] = a
        ws_ref[sl, :] = b
        ww_ref[sl, :] = e
        we_ref[sl, :] = f
        ok = (rok_ref[sl, :] > 0.5) & (cok_ref[...] > 0.5)
        inv = jnp.where(ok, 1.0 / (a + b + e + f + v_ref[rows_of(k + offset), :]), 0.0)
        inv_ref[sl, :] = inv
        if zero_start:
            buf_ref[sl, :] = jnp.where(inv != 0.0, l_ref[sl, :] * inv, 0.0)
        return carry

    lax.fori_loop(0, count, weights, 0, unroll=UNROLL)

    def sweep(src, dst):
        def body(k, carry):
            sl = rows_of(k)
            x = src[sl, :]
            summed = (
                l_ref[sl, :]
                + wn_ref[sl, :] * row_above(x, chunk(src, k - 1, count))
                + ws_ref[sl, :] * row_below(x, chunk(src, k + 1, count))
                + ww_ref[sl, :] * pltpu.roll(x, 1, 1)
                + we_ref[sl, :] * pltpu.roll(x, w - 1, 1)
            )
            inv = inv_ref[sl, :]
            dst[sl, :] = jnp.where(inv != 0.0, summed * inv, 0.0)
            return carry

        lax.fori_loop(0, count, body, 0, unroll=UNROLL)

    def first_sweep(k, carry):
        sl = rows_of(k)
        x = d_ref[rows_of(k + offset), :]
        summed = (
            l_ref[sl, :]
            + wn_ref[sl, :] * row_above(x, d_ref[rows_of(jnp.maximum(k - 1, 0) + offset), :])
            + ws_ref[sl, :] * row_below(x, d_ref[rows_of(jnp.minimum(k + 1, count - 1) + offset), :])
            + ww_ref[sl, :] * pltpu.roll(x, 1, 1)
            + we_ref[sl, :] * pltpu.roll(x, w - 1, 1)
        )
        inv = inv_ref[sl, :]
        buf_ref[sl, :] = jnp.where(inv != 0.0, summed * inv, 0.0)
        return carry

    if not zero_start:
        lax.fori_loop(0, count, first_sweep, 0, unroll=UNROLL)
    sweep(buf_ref, o_ref)
    sweep(o_ref, buf_ref)
    sweep(buf_ref, o_ref)


def run_power(drop, parts, row_ok, col_ok, offset=0):
    stacked = not isinstance(parts, (tuple, list))
    n, w = parts.shape[1:] if stacked else parts[0].shape
    operands = ([] if drop is None else [drop]) + ([parts] if stacked else list(parts)) + [row_ok, col_ok]
    kernel = functools.partial(power_kernel, zero_start=drop is None, stacked=stacked, offset=offset)
    return pl.pallas_call(
        kernel,
        out_shape=jax.ShapeDtypeStruct((n, w), jnp.float32),
        scratch_shapes=[pltpu.VMEM((n, w), jnp.float32) for _ in range(6)],
        compiler_params=pltpu.CompilerParams(vmem_limit_bytes=60 * 1024 * 1024),
        interpret=INTERPRET,
    )(*operands)


def thermal_kernel(*refs, stride, stored, zero_start):
    refs = list(refs)
    t_ref = None if zero_start else refs.pop(0)
    s_ref, lk_ref, vk_ref, rok_ref, o_ref = refs[:5]
    scratch = refs[5:]
    n, w = lk_ref.shape
    count = n // 8
    lane = lax.broadcasted_iota(jnp.int32, (8, w), 1)
    first = lane == 0
    last = lane == w - 1
    if stored:
        wn_ref, ws_ref, ww_ref, we_ref, wb_ref, wa_ref, inv_ref, buf_ref = scratch
    else:
        wb_ref, wa_ref, inv_ref, buf_ref = scratch

    def lateral(x, k, ref):
        up = row_above(x, chunk(ref, k - 1, count))
        dn = row_below(x, chunk(ref, k + 1, count))
        lf = jnp.where(first, 0.0, pltpu.roll(x, 1, 1))
        rt = jnp.where(last, 0.0, pltpu.roll(x, w - 1, 1))
        return up, dn, lf, rt

    def lateral_weights(k):
        sl = rows_of(k)
        x = lk_ref[sl, :]
        up, dn, lf, rt = lateral(x, k, lk_ref)
        return (x + up) * 0.5, (x + dn) * 0.5, (x + lf) * 0.5, (x + rt) * 0.5

    def weights(k, carry):
        sl = rows_of(k)
        a, b, e, f = lateral_weights(k)
        if stored:
            wn_ref[sl, :] = a
            ws_ref[sl, :] = b
            ww_ref[sl, :] = e
            we_ref[sl, :] = f
        v = vk_ref[sl, :]
        lo = (v + chunk(vk_ref, k - stride, count)) * 0.5
        hi = (v + chunk(vk_ref, k + stride, count)) * 0.5
        wb_ref[sl, :] = lo
        wa_ref[sl, :] = hi
        inv = jnp.where(rok_ref[sl, :] > 0.5, 1.0 / (a + b + e + f + lo + hi), 0.0)
        inv_ref[sl, :] = inv
        if zero_start:
            buf_ref[sl, :] = jnp.where(inv != 0.0, s_ref[sl, :] * inv, 0.0)
        return carry

    lax.fori_loop(0, count, weights, 0, unroll=UNROLL)

    def sweep(src, dst):
        def body(k, carry):
            sl = rows_of(k)
            if stored:
                a, b, e, f = wn_ref[sl, :], ws_ref[sl, :], ww_ref[sl, :], we_ref[sl, :]
            else:
                a, b, e, f = lateral_weights(k)
            x = src[sl, :]
            up, dn, lf, rt = lateral(x, k, src)
            summed = (
                s_ref[sl, :]
                + a * up
                + b * dn
                + e * lf
                + f * rt
                + wb_ref[sl, :] * chunk(src, k - stride, count)
                + wa_ref[sl, :] * chunk(src, k + stride, count)
            )
            inv = inv_ref[sl, :]
            dst[sl, :] = jnp.where(inv != 0.0, summed * inv, 0.0)
            return carry

        lax.fori_loop(0, count, body, 0, unroll=UNROLL)

    if not zero_start:
        sweep(t_ref, buf_ref)
    sweep(buf_ref, o_ref)
    sweep(o_ref, buf_ref)
    sweep(buf_ref, o_ref)


def run_thermal(temp, source, lat, vert, row_ok, stride):
    n, w = lat.shape
    stored = 13 * n * w * 4 <= 40 * 1024 * 1024
    kernel = functools.partial(thermal_kernel, stride=stride, stored=stored, zero_start=temp is None)
    return pl.pallas_call(
        kernel,
        out_shape=jax.ShapeDtypeStruct((n, w), jnp.float32),
        scratch_shapes=[pltpu.VMEM((n, w), jnp.float32) for _ in range(8 if stored else 4)],
        compiler_params=pltpu.CompilerParams(vmem_limit_bytes=60 * 1024 * 1024),
        interpret=INTERPRET,
    )(*([] if temp is None else [temp]), source, lat, vert, row_ok)


def inside_of(start, count, total):
    idx = start + jnp.arange(count, dtype=jnp.int32)
    return (idx >= 0) & (idx < total)


def body(demand, leakage, conductance, vias, layer_of, lateral_k, vertical_k):
    tile_rows, tile_cols = demand.shape
    group_layers, cell_rows, therm_cols = lateral_k.shape
    cell_cols = tile_cols // COARSE
    n_r = lax.axis_size("row")
    n_c = lax.axis_size("col")
    r_idx = lax.axis_index("row")
    c_idx = lax.axis_index("col")
    all_layers = group_layers * n_c
    all_rows = cell_rows * n_r
    total_rows = tile_rows * n_r
    total_cols = tile_cols * n_c

    T0 = 2 * HEAT_SWEEPS
    T1 = HEAT_SWEEPS
    H0 = T0 - 1
    H1 = T1 - 1
    S = SWEEPS
    R1 = H1 * COARSE + SWEEPS
    R0 = max(H0 * COARSE, R1) + SWEEPS
    CW = 64
    PR = -(-R1 // COARSE)
    PC = CW // COARSE

    via_g = VIA_CONDUCT * vias.astype(jnp.float32)
    load0 = demand + leakage

    p0 = extended(jnp.stack([conductance, load0, via_g]), (("row", 1, R0), ("col", 2, CW)))
    k_in, p0 = lax.optimization_barrier((jnp.stack([lateral_k, vertical_k]), p0))
    k_ext = extended(k_in, (("col", 1, T1), ("row", 2, T0)))

    cols_w = tile_cols + 2 * CW
    col_ok = inside_of(c_idx * tile_cols - CW, cols_w, total_cols).astype(jnp.float32)[None, :]

    rows0 = tile_rows + 2 * R0
    row_ok0 = inside_of(r_idx * tile_rows - R0, rows0, total_rows).astype(jnp.float32)[:, None]
    drop0 = run_power(None, p0, row_ok0, col_ok)
    p1_in, layer_in, drop0 = lax.optimization_barrier((jnp.stack([demand, leakage]), layer_of, drop0))
    p1 = extended(p1_in, (("row", 1, R1), ("col", 2, CW)))
    layer_ext = extended(layer_in, (("row", 0, T0),))
    hr0 = H0 * COARSE
    rs = slice(R0 - hr0, R0 + tile_rows + hr0)
    cs = slice(CW, CW + tile_cols)
    d_h = drop0[rs, cs]
    heat0 = coarse_of(p0[1][rs, cs] * (1.0 - d_h) + p0[0][rs, cs] * d_h * d_h)

    def gather_heat(heat):
        copies = jnp.broadcast_to(heat[None], (n_c,) + heat.shape)
        gathered = lax.all_to_all(copies, "col", split_axis=0, concat_axis=0, tiled=True)
        gathered = gathered.transpose(1, 0, 2).reshape(heat.shape[0], n_c * cell_cols)
        return jnp.pad(gathered, ((1, 1), (0, 0)))

    def thermal(temp_ext, heat_ext, halo):
        layers = group_layers + 2 * T1
        rows = cell_rows + 2 * halo
        ks = k_ext[:, :, T0 - halo:T0 + cell_rows + halo]
        tlay = c_idx * group_layers - T1 + jnp.arange(layers, dtype=jnp.int32)
        inside = inside_of(c_idx * group_layers - T1, layers, all_layers)[:, None] & inside_of(r_idx * cell_rows - halo, rows, all_rows)[None, :]
        lay_in = layer_ext[T0 - halo:T0 + cell_rows + halo]
        picker = (lay_in[None, :, :] == tlay[:, None, None]) & inside[:, :, None]
        source = jnp.where(picker, heat_ext[None, :, :], 0.0)
        flat = (layers * rows, therm_cols)
        out = run_thermal(
            None if temp_ext is None else temp_ext.reshape(flat), source.reshape(flat), ks[0].reshape(flat), ks[1].reshape(flat),
            inside.astype(jnp.float32).reshape(layers * rows, 1), rows // 8,
        )
        return out.reshape(layers, rows, therm_cols)

    temp0 = thermal(None, gather_heat(heat0), T0)
    temp0 = temp0[T1:T1 + group_layers, T0 - T1:T0 + cell_rows + T1]

    own_layers = c_idx * group_layers + jnp.arange(group_layers, dtype=jnp.int32)
    t_own = temp0[:, T1 - PR:T1 + cell_rows + PR]
    lay_w = layer_ext[T0 - PR:T0 + cell_rows + PR]
    partial = jnp.sum(jnp.where(lay_w[None, :, :] == own_layers[:, None, None], t_own, 0.0), axis=0)
    partial = jnp.pad(partial, ((0, 0), (PC, PC)))
    windows = jnp.stack([partial[:, j * cell_cols:j * cell_cols + cell_cols + 2 * PC] for j in range(n_c)])
    windows = lax.all_to_all(windows, "col", split_axis=0, concat_axis=0, tiled=True)
    cell_temp = jnp.sum(windows, axis=0)

    denom_c = 1.0 + COND_SLOPE * cell_temp
    grow_c = jnp.exp(LEAK_SLOPE * cell_temp)
    rows1 = tile_rows + 2 * R1
    fo = PR * COARSE - R1
    denom_f = fine_of(denom_c, cols_w)[fo:fo + rows1]
    grow_f = fine_of(grow_c, cols_w)[fo:fo + rows1]
    rs1 = slice(R0 - R1, R0 - R1 + rows1)
    cond1 = p0[0][rs1] / denom_f
    load1 = p1[0] + p1[1] * grow_f
    row_ok1 = inside_of(r_idx * tile_rows - R1, rows1, total_rows).astype(jnp.float32)[:, None]
    drop1 = run_power(drop0, (cond1, load1, p0), row_ok1, col_ok, offset=(R0 - R1) // 8)
    hr1 = H1 * COARSE
    rh = slice(R1 - hr1, R1 + tile_rows + hr1)
    d_h1 = drop1[rh, cs]
    heat1 = coarse_of(load1[rh, cs] * (1.0 - d_h1) + cond1[rh, cs] * d_h1 * d_h1)
    temp1 = thermal(extended(temp0, (("col", 0, T1),)), gather_heat(heat1), T1)
    temp_out = temp1[T1:T1 + group_layers, T1:T1 + cell_rows]
    drop_out = drop1[R1:R1 + tile_rows, cs]
    return (drop_out, temp_out)


def solution(mesh):
    in_specs = (
        P("row", "col"),
        P("row", "col"),
        P("row", "col"),
        P("row", "col"),
        P("row", None),
        P("col", "row", None),
        P("col", "row", None),
    )
    out_specs = (P("row", "col"), P("col", "row", None))
    return jax.shard_map(body, mesh=mesh, in_specs=in_specs, out_specs=out_specs, check_vma=False)
```

profile of v0, /device:TPU:8, one launch (start us, length us, event | category | flops | bytes accessed | tf_op | source)
XLA Modules:
  0.0 212.4 jit_solution(12768942187839525126)
XLA Ops:
  0.6 2.2 %multiply_bitcast_fusion = (f32[1,256,1024]{2,1,0:T(8,128)S(1)}, f32[1,256,1024]{2,1,0:T(8,128)S(1)}) fusion(s32[256,1024]{1,0:T(8,128)} %param.10, f32[256,1024]{1,0:T(8,128)} %param.7, f32[256,1024]{1,0:T(8,128)} %param.8), kind=kLoop, calls=%fused_computation.31 | loop fusion | flops 786432 | bytes 5242880 | tf_op jit(solution)/shard_map/stack | solution.py:293
  2.9 1.5 pad_maximum_fusion.8
  4.4 2.1 collective-permute-start
  6.5 3.6 %collective-permute-start.1 = (f32[3,60,1024]{2,1,0:T(8,128)}, f32[3,60,1024]{2,1,0:T(8,128)}, u32[]{:S(2)}, u32[]{:S(2)}) collective-permute-start(f32[3,60,1024]{2,1,0:T(8,128)} %get-tuple-element.21), channel_id=1, source_target_pairs={{4,0},{8,4},{12,8},{16,12},{20,16},{24,20},{28,24},{5,1},{9,5},{13... | collective-permute-start | bytes 2211848 | tf_op jit(solution)/shard_map/ppermute | solution.py:35
  11.3 0.9 reshape.277.refs_3_
  13.3 0.9 reshape.278.refs_4_
  16.0 0.7 fusion.22.refs_4_
  16.7 0.7 fusion.18.refs_1_
  17.4 1.1 pad_maximum_fusion.5
  18.5 1.8 pad_maximum_fusion.3
  20.6 2.4 %pad_maximum_fusion = f32[3,376,1024]{2,1,0:T(8,128)S(1)} fusion(f32[3,60,1024]{2,1,0:T(8,128)} %collective-permute-done.1, f32[1,256,1024]{2,1,0:T(8,128)S(1)} %get-tuple-element.40, f32[1,256,1024]{2,1,0:T(8,128)S(1)} %copy-done.7, f32[1,256,1024]{2,1,0:T(8,128)S(1)} %bitcast.90, f32[3,60,1024]{2,1,0:T(8,128)} %collective-permute-done), kind=kLoop, calls=%fused_computation | loop fusion | flops 4620288 | bytes 9240576 | tf_op jit(solution)/shard_map/concatenate | solution.py:36
  23.1 2.1 %copy-done = f32[3,376,1024]{2,1,0:T(8,128)} copy-done((f32[3,376,1024]{2,1,0:T(8,128)}, f32[3,376,1024]{2,1,0:T(8,128)S(1)}, u32[]{:S(2)}) %copy-start) | copy-done | bytes 4620312
  25.7 3.4 %collective-permute-start.2 = (f32[3,376,64]{1,2,0:T(8,128)S(1)}, f32[3,376,64]{1,2,0:T(8,128)S(1)}, u32[]{:S(2)}, u32[]{:S(2)}) collective-permute-start(f32[3,376,64]{1,2,0:T(8,128)S(1)} %copy.33), channel_id=1, source_target_pairs={{0,1},{1,2},{2,3},{4,5},{5,6},{6,7},{8,9},{9,10},{10,11},{12,13},{... | collective-permute-start | bytes 866312 | tf_op jit(solution)/shard_map/ppermute | solution.py:32
  29.1 0.9 copy.34
  30.0 1.3 collective-permute-start.3
  32.5 3.8 %collective-permute-done.2 = f32[3,376,64]{1,2,0:T(8,128)S(1)} collective-permute-done((f32[3,376,64]{1,2,0:T(8,128)S(1)}, f32[3,376,64]{1,2,0:T(8,128)S(1)}, u32[]{:S(2)}, u32[]{:S(2)}) %collective-permute-start.2) | collective-permute-done | bytes 288800 | tf_op jit(solution)/shard_map/ppermute | solution.py:32
  36.5 8.1 %collective-permute-done.3 = f32[3,376,64]{1,2,0:T(8,128)} collective-permute-done((f32[3,376,64]{1,2,0:T(8,128)}, f32[3,376,64]{1,2,0:T(8,128)}, u32[]{:S(2)}, u32[]{:S(2)}) %collective-permute-start.3) | collective-permute-done | bytes 288800 | tf_op jit(solution)/shard_map/ppermute | solution.py:35
  44.6 1.2 copy.36
  45.8 6.9 %concatenate.25.refs_0_.refs_3_ = f32[3,376,1152]{2,1,0:T(8,128)} concatenate(f32[3,376,64]{2,1,0:T(8,128)S(1)} %copy.35, f32[3,376,1024]{2,1,0:T(8,128)} %copy-done, f32[3,376,64]{2,1,0:T(8,128)S(1)} %copy.36), dimensions={2} | concatenate | bytes 10395648 | tf_op jit(solution)/shard_map/concatenate | solution.py:36
  52.7 4.0 %slice_bitcast_fusion.1 = (f32[376,1152]{1,0:T(8,128)}, f32[376,1152]{1,0:T(8,128)}) fusion(f32[3,376,1152]{2,1,0:T(8,128)} %concatenate.25.refs_0_.refs_3_), kind=kLoop, calls=%fused_computation.7 | loop fusion | bytes 6930432 | tf_op jit(solution)/shard_map/squeeze | solution.py:310
  56.7 12.7 %shard_map.86.refs_0_ = f32[376,1152]{1,0:T(8,128)} custom-call(f32[3,376,1152]{2,1,0:T(8,128)} %concatenate.25.refs_0_.refs_3_, f32[376,1]{1,0:T(8,128)} %fusion.18.refs_1_, f32[1,1152]{1,0:T(1,128)} %and_convert_fusion.refs_2_.refs_5_), custom_call_target="tpu_custom_call" | custom-call | tf_op jit(solution)/shard_map/pallas_call | solution.py:159
  69.4 0.9 fusion.45
  70.3 1.9 collective-permute-start.10
  72.2 3.6 %collective-permute-start.11 = (f32[2,28,1024]{2,1,0:T(8,128)}, f32[2,28,1024]{2,1,0:T(8,128)}, u32[]{:S(2)}, u32[]{:S(2)}) collective-permute-start(f32[2,28,1024]{2,1,0:T(8,128)} %get-tuple-element.25), channel_id=1, source_target_pairs={{4,0},{8,4},{12,8},{16,12},{20,16},{24,20},{28,24},{5,1},{9,5},{13... | collective-permute-start | bytes 688136 | tf_op jit(solution)/shard_map/ppermute | solution.py:35
  76.0 3.4 %collective-permute-start.6 = (f32[2,4,32,512]{3,2,1,0:T(8,128)S(1)}, f32[2,4,32,512]{3,2,1,0:T(8,128)S(1)}, u32[]{:S(2)}, u32[]{:S(2)}) collective-permute-start(f32[2,4,32,512]{3,2,1,0:T(8,128)S(1)} %get-tuple-element.33), channel_id=1, source_target_pairs={{0,1},{1,2},{2,3},{4,5},{5,6},{6,7},{8,9},{9,10},{10,11},{12,13},{... | collective-permute-start | bytes 1572872 | tf_op jit(solution)/shard_map/ppermute | solution.py:32
  79.4 1.3 collective-permute-start.7
  80.7 1.9 collective-permute-start.4
  82.7 3.4 %fusion.3 = f32[46,1024]{1,0:T(8,128)S(1)} fusion(f32[376,1152]{1,0:T(8,128)} %get-tuple-element.13, f32[376,1152]{1,0:T(8,128)} %get-tuple-element.12, f32[376,1152]{1,0:T(8,128)S(1)} %copy-done.1), kind=kLoop, calls=%fused_computation.13 | loop fusion | flops 2213888 | bytes 4710400 | tf_op jit(solution)/shard_map/reduce_sum | solution.py:55
  87.1 3.9 %all-to-all-start = ((f32[4,46,128]{2,1,0:T(8,128)}), f32[4,46,128]{2,1,0:T(8,128)S(1)}, u32[]{:S(2)}, u32[]{:S(2)}) async-start(f32[4,46,128]{2,1,0:T(8,128)} %broadcast_in_dim.36), calls=%async_computation | async-start | bytes 196608 | tf_op jit(solution)/shard_map/all_to_all | solution.py:314
  91.0 3.4 %collective-permute-start.5 = (s32[8,512]{1,0:T(8,128)S(1)}, s32[8,512]{1,0:T(8,128)S(1)}, u32[]{:S(2)}, u32[]{:S(2)}) collective-permute-start(s32[8,512]{1,0:T(8,128)S(1)} %get-tuple-element.38), channel_id=1, source_target_pairs={{4,0},{8,4},{12,8},{16,12},{20,16},{24,20},{28,24},{5,1},{9,5},{13... | collective-permute-start | bytes 49160 | tf_op jit(solution)/shard_map/ppermute | solution.py:35
  94.6 8.6 %collective-permute-done.7 = f32[2,4,32,512]{3,2,1,0:T(8,128)S(1)} collective-permute-done((f32[2,4,32,512]{3,2,1,0:T(8,128)S(1)}, f32[2,4,32,512]{3,2,1,0:T(8,128)S(1)}, u32[]{:S(2)}, u32[]{:S(2)}) %collective-permute-start.7) | collective-permute-done | bytes 524320 | tf_op jit(solution)/shard_map/ppermute | solution.py:35
  103.2 1.2 fusion.46
  104.4 1.9 collective-permute-start.8
  106.4 3.6 %collective-permute-start.9 = (f32[2,16,8,512]{3,2,1,0:T(8,128)}, f32[2,16,8,512]{3,2,1,0:T(8,128)}, u32[]{:S(2)}, u32[]{:S(2)}) collective-permute-start(f32[2,16,8,512]{3,2,1,0:T(8,128)} %get-tuple-element.27), channel_id=1, source_target_pairs={{4,0},{8,4},{12,8},{16,12},{20,16},{24,20},{28,24},{5,1},{9,5},{13... | collective-permute-start | bytes 1572872 | tf_op jit(solution)/shard_map/ppermute | solution.py:35
  110.1 1.3 pad_maximum_fusion.2
  111.4 0.9 fusion.44
  112.3 2.2 %collective-permute-start.12 = (f32[2,312,64]{2,1,0:T(8,128)}, f32[2,312,64]{2,1,0:T(8,128)}, u32[]{:S(2)}, u32[]{:S(2)}) collective-permute-start(f32[2,312,64]{2,1,0:T(8,128)} %get-tuple-element.23), channel_id=1, source_target_pairs={{0,1},{1,2},{2,3},{4,5},{5,6},{6,7},{8,9},{9,10},{10,11},{12,13},{... | collective-permute-start | bytes 479240 | tf_op jit(solution)/shard_map/ppermute | solution.py:32
  114.5 1.3 collective-permute-start.13
  116.0 1.6 bitcast_select_fusion.refs_0_
  117.6 2.4 %collective-permute-done.12 = f32[2,312,64]{2,1,0:T(8,128)} collective-permute-done((f32[2,312,64]{2,1,0:T(8,128)}, f32[2,312,64]{2,1,0:T(8,128)}, u32[]{:S(2)}, u32[]{:S(2)}) %collective-permute-start.12) | collective-permute-done | bytes 159776 | tf_op jit(solution)/shard_map/ppermute | solution.py:32
  120.0 7.5 %collective-permute-done.13 = f32[2,312,64]{2,1,0:T(8,128)} collective-permute-done((f32[2,312,64]{2,1,0:T(8,128)}, f32[2,312,64]{2,1,0:T(8,128)}, u32[]{:S(2)}, u32[]{:S(2)}) %collective-permute-start.13) | collective-permute-done | bytes 159776 | tf_op jit(solution)/shard_map/ppermute | solution.py:35
  127.5 3.8 %concatenate.30 = f32[2,312,1152]{2,1,0:T(8,128)} concatenate(f32[2,312,64]{2,1,0:T(8,128)} %collective-permute-done.12, f32[2,312,1024]{2,1,0:T(8,128)S(1)} %pad_maximum_fusion.2, f32[2,312,64]{2,1,0:T(8,128)} %collective-permute-done.13), dimensions={2} | concatenate | bytes 5750784 | tf_op jit(solution)/shard_map/concatenate | solution.py:36
  131.4 0.8 copy-done.13
  132.2 2.3 %pad_maximum_fusion.1 = f32[2,16,48,512]{3,2,1,0:T(8,128)S(1)} fusion(f32[2,16,8,512]{3,2,1,0:T(8,128)} %collective-permute-done.9, f32[2,16,32,512]{3,2,1,0:T(8,128)} %copy-done.9, f32[2,16,8,512]{3,2,1,0:T(8,128)} %copy-done.13), kind=kLoop, calls=%fused_computation.1 | loop fusion | flops 1572864 | bytes 6291456 | tf_op jit(solution)/shard_map/concatenate | solution.py:36
  134.5 2.0 fusion.43
  136.5 11.0 %shard_map.87 = f32[768,512]{1,0:T(8,128)} custom-call(f32[768,512]{1,0:T(8,128)} %bitcast_select_fusion.refs_0_, f32[768,512]{1,0:T(8,128)} %bitcast.81, f32[768,512]{1,0:T(8,128)} %bitcast.80, f32[768,1]{1,0:T(8,128)} %reshape.277.refs_3_), custom_call_target="tpu_custom_call" | custom-call | tf_op jit(solution)/shard_map/pallas_call | solution.py:252
  147.5 2.1 fusion.48
  149.7 0.7 pad_maximum_fusion.9
  150.4 3.3 %all-to-all-start.1 = ((f32[4,40,144]{2,1,0:T(8,128)}), f32[4,40,144]{2,1,0:T(8,128)S(1)}, u32[]{:S(2)}, u32[]{:S(2)}) async-start(f32[4,40,144]{2,1,0:T(8,128)} %pad_maximum_fusion.9), calls=%async_computation.1 | async-start | bytes 327680 | tf_op jit(solution)/shard_map/all_to_all | solution.py:343
  153.7 2.0 fusion.47
  155.8 4.6 %collective-permute-start.14 = (f32[4,40,512]{2,1,0:T(8,128)}, f32[4,40,512]{2,1,0:T(8,128)}, u32[]{:S(2)}, u32[]{:S(2)}) collective-permute-start(f32[4,40,512]{2,1,0:T(8,128)} %get-tuple-element.28), channel_id=1, source_target_pairs={{0,1},{1,2},{2,3},{4,5},{5,6},{6,7},{8,9},{9,10},{10,11},{12,13},{... | collective-permute-start | bytes 983048 | tf_op jit(solution)/shard_map/ppermute | solution.py:32
  160.4 1.5 collective-permute-start.15
  162.8 2.9 %slice_divide_fusion.refs_1_ = f32[312,1152]{1,0:T(8,128)} fusion(f32[320,1152]{1,0:T(8,128)S(1)} %broadcast_bitcast_fusion.1, f32[3,376,1152]{2,1,0:T(8,128)} %concatenate.25.refs_0_.refs_3_), kind=kLoop, calls=%fused_computation.19 | loop fusion | flops 359424 | bytes 4313088 | tf_op jit(solution)/shard_map/div | solution.py:353
  165.7 1.5 fusion.4.refs_2_
  167.2 14.3 %shard_map.88 = f32[312,1152]{1,0:T(8,128)} custom-call(f32[376,1152]{1,0:T(8,128)} %shard_map.86.refs_0_, f32[312,1152]{1,0:T(8,128)} %slice_divide_fusion.refs_1_, f32[312,1152]{1,0:T(8,128)} %fusion.4.refs_2_, f32[3,376,1152]{2,1,0:T(8,128)} %concatenate.25.refs_0_.refs_3_, f32[312,1]{1,0:T(8,128)} %fusion.22.refs_4_, ...), custom_call_target="tpu_custom_call" | custom-call | tf_op jit(solution)/shard_map/pallas_call | solution.py:159
  181.5 3.4 %fusion.8 = f32[38,1024]{1,0:T(8,128)S(1)} fusion(f32[312,1152]{1,0:T(8,128)} %slice_divide_fusion.refs_1_, f32[312,1152]{1,0:T(8,128)} %fusion.4.refs_2_, f32[312,1152]{1,0:T(8,128)} %shard_map.88), kind=kLoop, calls=%fused_computation.26 | loop fusion | flops 1828864 | bytes 3891200 | tf_op jit(solution)/shard_map/reduce_sum | solution.py:55
  185.9 4.6 %all-to-all-start.2 = ((f32[4,38,128]{2,1,0:T(8,128)}), f32[4,38,128]{2,1,0:T(8,128)S(1)}, u32[]{:S(2)}, u32[]{:S(2)}) async-start(f32[4,38,128]{2,1,0:T(8,128)} %broadcast_in_dim.43), calls=%async_computation.2 | async-start | bytes 163840 | tf_op jit(solution)/shard_map/all_to_all | solution.py:314
  190.6 2.0 fusion.42
  192.6 1.3 slice.196
  193.9 1.6 all-to-all-done.2
  195.5 1.4 bitcast_select_fusion.1.refs_1_
  197.0 2.3 %pad_maximum_fusion.4 = f32[16,40,512]{2,1,0:T(8,128)} fusion(f32[4,40,512]{2,1,0:T(8,128)} %collective-permute-done.15, f32[8,40,512]{2,1,0:T(8,128)S(1)} %copy-done.12, f32[4,40,512]{2,1,0:T(8,128)} %collective-permute-done.14), kind=kLoop, calls=%fused_computation.20 | loop fusion | flops 655360 | bytes 2621440 | tf_op jit(solution)/shard_map/concatenate | solution.py:36
  199.3 11.2 %shard_map.89 = f32[640,512]{1,0:T(8,128)} custom-call(f32[640,512]{1,0:T(8,128)} %bitcast.86, f32[640,512]{1,0:T(8,128)} %bitcast_select_fusion.1.refs_1_, f32[640,512]{1,0:T(8,128)} %bitcast.85, f32[640,512]{1,0:T(8,128)} %bitcast.84, f32[640,1]{1,0:T(8,128)} %reshape.278.refs_4_), custom_call_target="tpu_custom_call" | custom-call | tf_op jit(solution)/shard_map/pallas_call | solution.py:252
  210.5 1.9 slice.204
  (111 shorter events, 9.8 us)
Async XLA Ops:
  0.6 2.3 %copy-start.10 = (f32[256,1024]{1,0:T(8,128)S(1)}, f32[256,1024]{1,0:T(8,128)}, u32[]{:S(2)}) copy-start(f32[256,1024]{1,0:T(8,128)} %param.9) | copy-start | bytes 3145732
  2.9 1.6 copy-start.6
  4.4 13.0 %copy-start.14 = (f32[8,32,512]{2,1,0:T(8,128)S(1)}, f32[8,32,512]{2,1,0:T(8,128)}, u32[]{:S(2)}) copy-start(f32[8,32,512]{2,1,0:T(8,128)} %param.13) | copy-start | bytes 1572868
  4.4 13.0 %copy-start.15 = (f32[8,32,512]{2,1,0:T(8,128)S(1)}, f32[8,32,512]{2,1,0:T(8,128)}, u32[]{:S(2)}) copy-start(f32[8,32,512]{2,1,0:T(8,128)} %param.12) | copy-start | bytes 1572868
  4.4 15.9 %collective-permute-start = (f32[3,60,1024]{2,1,0:T(8,128)}, f32[3,60,1024]{2,1,0:T(8,128)}, u32[]{:S(2)}, u32[]{:S(2)}) collective-permute-start(f32[3,60,1024]{2,1,0:T(8,128)} %get-tuple-element.20), channel_id=1, source_target_pairs={{0,4},{4,8},{8,12},{12,16},{16,20},{20,24},{24,28},{1,5},{5,9},{9,... | collective-permute-start | bytes 2211848 | tf_op jit(solution)/shard_map/ppermute | solution.py:32
  6.5 13.8 %collective-permute-start.1 = (f32[3,60,1024]{2,1,0:T(8,128)}, f32[3,60,1024]{2,1,0:T(8,128)}, u32[]{:S(2)}, u32[]{:S(2)}) collective-permute-start(f32[3,60,1024]{2,1,0:T(8,128)} %get-tuple-element.21), channel_id=1, source_target_pairs={{4,0},{8,4},{12,8},{16,12},{20,16},{24,20},{28,24},{5,1},{9,5},{13... | collective-permute-start | bytes 2211848 | tf_op jit(solution)/shard_map/ppermute | solution.py:35
  18.5 1.9 copy-start.7
  18.5 2.2 %copy-start.11 = (f32[256,1024]{1,0:T(8,128)S(1)}, f32[256,1024]{1,0:T(8,128)}, u32[]{:S(2)}) copy-start(f32[256,1024]{1,0:T(8,128)} %param.9) | copy-start | bytes 3145732
  20.3 49.1 %copy-start.3 = (f32[2,256,1024]{2,1,0:T(8,128)}, f32[2,256,1024]{2,1,0:T(8,128)S(1)}, u32[]{:S(2)}) copy-start(f32[2,256,1024]{2,1,0:T(8,128)S(1)} %pad_maximum_fusion.3) | copy-start | bytes 6291460
  23.1 2.1 %copy-start = (f32[3,376,1024]{2,1,0:T(8,128)}, f32[3,376,1024]{2,1,0:T(8,128)S(1)}, u32[]{:S(2)}) copy-start(f32[3,376,1024]{2,1,0:T(8,128)S(1)} %pad_maximum_fusion) | copy-start | bytes 13860868
  25.7 10.6 %collective-permute-start.2 = (f32[3,376,64]{1,2,0:T(8,128)S(1)}, f32[3,376,64]{1,2,0:T(8,128)S(1)}, u32[]{:S(2)}, u32[]{:S(2)}) collective-permute-start(f32[3,376,64]{1,2,0:T(8,128)S(1)} %copy.33), channel_id=1, source_target_pairs={{0,1},{1,2},{2,3},{4,5},{5,6},{6,7},{8,9},{9,10},{10,11},{12,13},{... | collective-permute-start | bytes 866312 | tf_op jit(solution)/shard_map/ppermute | solution.py:32
  30.0 14.6 %collective-permute-start.3 = (f32[3,376,64]{1,2,0:T(8,128)}, f32[3,376,64]{1,2,0:T(8,128)}, u32[]{:S(2)}, u32[]{:S(2)}) collective-permute-start(f32[3,376,64]{1,2,0:T(8,128)} %copy.34), channel_id=1, source_target_pairs={{1,0},{2,1},{3,2},{5,4},{6,5},{7,6},{9,8},{10,9},{11,10},{13,12},{... | collective-permute-start | bytes 866312 | tf_op jit(solution)/shard_map/ppermute | solution.py:35
  56.7 19.1 %copy-start.8 = (f32[2,8,32,512]{3,2,1,0:T(8,128)S(1)}, f32[2,8,32,512]{3,2,1,0:T(8,128)}, u32[]{:S(2)}) copy-start(f32[2,8,32,512]{3,2,1,0:T(8,128)} %pad_maximum_fusion.5) | copy-start | bytes 3145732
  69.4 11.3 %copy-start.16 = (s32[32,512]{1,0:T(8,128)S(1)}, s32[32,512]{1,0:T(8,128)}, u32[]{:S(2)}) copy-start(s32[32,512]{1,0:T(8,128)} %param.11) | copy-start | bytes 196612
  69.4 13.3 %copy-start.1 = (f32[376,1152]{1,0:T(8,128)S(1)}, f32[376,1152]{1,0:T(8,128)}, u32[]{:S(2)}) copy-start(f32[376,1152]{1,0:T(8,128)} %shard_map.86.refs_0_) | copy-start | bytes 5197828
  70.3 39.7 %collective-permute-start.10 = (f32[2,28,1024]{2,1,0:T(8,128)}, f32[2,28,1024]{2,1,0:T(8,128)}, u32[]{:S(2)}, u32[]{:S(2)}) collective-permute-start(f32[2,28,1024]{2,1,0:T(8,128)} %get-tuple-element.24), channel_id=1, source_target_pairs={{0,4},{4,8},{8,12},{12,16},{16,20},{20,24},{24,28},{1,5},{5,9},{9,... | collective-permute-start | bytes 688136 | tf_op jit(solution)/shard_map/ppermute | solution.py:32
  72.2 37.8 %collective-permute-start.11 = (f32[2,28,1024]{2,1,0:T(8,128)}, f32[2,28,1024]{2,1,0:T(8,128)}, u32[]{:S(2)}, u32[]{:S(2)}) collective-permute-start(f32[2,28,1024]{2,1,0:T(8,128)} %get-tuple-element.25), channel_id=1, source_target_pairs={{4,0},{8,4},{12,8},{16,12},{20,16},{24,20},{28,24},{5,1},{9,5},{13... | collective-permute-start | bytes 688136 | tf_op jit(solution)/shard_map/ppermute | solution.py:35
  76.0 18.4 %collective-permute-start.6 = (f32[2,4,32,512]{3,2,1,0:T(8,128)S(1)}, f32[2,4,32,512]{3,2,1,0:T(8,128)S(1)}, u32[]{:S(2)}, u32[]{:S(2)}) collective-permute-start(f32[2,4,32,512]{3,2,1,0:T(8,128)S(1)} %get-tuple-element.33), channel_id=1, source_target_pairs={{0,1},{1,2},{2,3},{4,5},{5,6},{6,7},{8,9},{9,10},{10,11},{12,13},{... | collective-permute-start | bytes 1572872 | tf_op jit(solution)/shard_map/ppermute | solution.py:32
  79.4 23.8 %collective-permute-start.7 = (f32[2,4,32,512]{3,2,1,0:T(8,128)S(1)}, f32[2,4,32,512]{3,2,1,0:T(8,128)S(1)}, u32[]{:S(2)}, u32[]{:S(2)}) collective-permute-start(f32[2,4,32,512]{3,2,1,0:T(8,128)S(1)} %get-tuple-element.32), channel_id=1, source_target_pairs={{1,0},{2,1},{3,2},{5,4},{6,5},{7,6},{9,8},{10,9},{11,10},{13,12},{... | collective-permute-start | bytes 1572872 | tf_op jit(solution)/shard_map/ppermute | solution.py:35
  80.7 10.3 %collective-permute-start.4 = (s32[8,512]{1,0:T(8,128)S(1)}, s32[8,512]{1,0:T(8,128)S(1)}, u32[]{:S(2)}, u32[]{:S(2)}) collective-permute-start(s32[8,512]{1,0:T(8,128)S(1)} %get-tuple-element.39), channel_id=1, source_target_pairs={{0,4},{4,8},{8,12},{12,16},{16,20},{20,24},{24,28},{1,5},{5,9},{9,... | collective-permute-start | bytes 49160 | tf_op jit(solution)/shard_map/ppermute | solution.py:32
  82.7 3.4 %copy-start.17 = (s32[1024]{0:T(1024)S(1)}, s32[1024]{0:T(1024)}, u32[]{:S(2)}) copy-start(s32[1024]{0:T(1024)} %add_select_fusion.1) | copy-start | bytes 12292
  87.1 28.8 %all-to-all-start = ((f32[4,46,128]{2,1,0:T(8,128)}), f32[4,46,128]{2,1,0:T(8,128)S(1)}, u32[]{:S(2)}, u32[]{:S(2)}) async-start(f32[4,46,128]{2,1,0:T(8,128)} %broadcast_in_dim.36), calls=%async_computation | async-start | bytes 196608 | tf_op jit(solution)/shard_map/all_to_all | solution.py:314
  91.0 24.8 %collective-permute-start.5 = (s32[8,512]{1,0:T(8,128)S(1)}, s32[8,512]{1,0:T(8,128)S(1)}, u32[]{:S(2)}, u32[]{:S(2)}) collective-permute-start(s32[8,512]{1,0:T(8,128)S(1)} %get-tuple-element.38), channel_id=1, source_target_pairs={{4,0},{8,4},{12,8},{16,12},{20,16},{24,20},{28,24},{5,1},{9,5},{13... | collective-permute-start | bytes 49160 | tf_op jit(solution)/shard_map/ppermute | solution.py:35
  94.6 15.5 %copy-start.4 = (f32[2,256,1024]{2,1,0:T(8,128)S(1)}, f32[2,256,1024]{2,1,0:T(8,128)}, u32[]{:S(2)}) copy-start(f32[2,256,1024]{2,1,0:T(8,128)} %copy-done.3) | copy-start | bytes 6291460
  103.2 6.8 %copy-start.9 = (f32[2,16,32,512]{3,2,1,0:T(8,128)}, f32[2,16,32,512]{3,2,1,0:T(8,128)S(1)}, u32[]{:S(2)}) copy-start(f32[2,16,32,512]{3,2,1,0:T(8,128)S(1)} %constant_dynamic-update-slice_fusion.3) | copy-start | bytes 6291460
  104.4 26.9 %collective-permute-start.8 = (f32[2,16,8,512]{3,2,1,0:T(8,128)}, f32[2,16,8,512]{3,2,1,0:T(8,128)S(1)}, u32[]{:S(2)}, u32[]{:S(2)}) collective-permute-start(f32[2,16,8,512]{3,2,1,0:T(8,128)} %get-tuple-element.26), channel_id=1, source_target_pairs={{0,4},{4,8},{8,12},{12,16},{16,20},{20,24},{24,28},{1,5},{5,9},{9,... | collective-permute-start | bytes 1572872 | tf_op jit(solution)/shard_map/ppermute | solution.py:32
  106.4 25.8 %collective-permute-start.9 = (f32[2,16,8,512]{3,2,1,0:T(8,128)}, f32[2,16,8,512]{3,2,1,0:T(8,128)}, u32[]{:S(2)}, u32[]{:S(2)}) collective-permute-start(f32[2,16,8,512]{3,2,1,0:T(8,128)} %get-tuple-element.27), channel_id=1, source_target_pairs={{4,0},{8,4},{12,8},{16,12},{20,16},{24,20},{28,24},{5,1},{9,5},{13... | collective-permute-start | bytes 1572872 | tf_op jit(solution)/shard_map/ppermute | solution.py:35
  111.4 4.6 %copy-start.19 = (s32[768]{0:T(1024)S(1)}, s32[768]{0:T(1024)}, u32[]{:S(2)}) copy-start(s32[768]{0:T(1024)} %eq.111) | copy-start | bytes 9220
  111.4 4.6 %copy-start.21 = (pred[768]{0:T(1024)(128)(4,1)S(1)}, pred[768]{0:T(1024)(128)(4,1)}, u32[]{:S(2)}) copy-start(pred[768]{0:T(1024)(128)(4,1)} %and.178) | copy-start | bytes 2308
  112.3 7.7 %collective-permute-start.12 = (f32[2,312,64]{2,1,0:T(8,128)}, f32[2,312,64]{2,1,0:T(8,128)}, u32[]{:S(2)}, u32[]{:S(2)}) collective-permute-start(f32[2,312,64]{2,1,0:T(8,128)} %get-tuple-element.23), channel_id=1, source_target_pairs={{0,1},{1,2},{2,3},{4,5},{5,6},{6,7},{8,9},{9,10},{10,11},{12,13},{... | collective-permute-start | bytes 479240 | tf_op jit(solution)/shard_map/ppermute | solution.py:32
  114.5 13.0 %collective-permute-start.13 = (f32[2,312,64]{2,1,0:T(8,128)}, f32[2,312,64]{2,1,0:T(8,128)}, u32[]{:S(2)}, u32[]{:S(2)}) collective-permute-start(f32[2,312,64]{2,1,0:T(8,128)} %get-tuple-element.22), channel_id=1, source_target_pairs={{1,0},{2,1},{3,2},{5,4},{6,5},{7,6},{9,8},{10,9},{11,10},{13,12},{... | collective-permute-start | bytes 479240 | tf_op jit(solution)/shard_map/ppermute | solution.py:35
  131.4 0.8 copy-start.13
  136.5 11.0 %copy-start.22 = (s32[8]{0:T(128)S(1)}, s32[8]{0:T(128)}, u32[]{:S(2)}) copy-start(s32[8]{0:T(128)} %iota_add_fusion.3) | copy-start | bytes 100
  150.4 11.5 %all-to-all-start.1 = ((f32[4,40,144]{2,1,0:T(8,128)}), f32[4,40,144]{2,1,0:T(8,128)S(1)}, u32[]{:S(2)}, u32[]{:S(2)}) async-start(f32[4,40,144]{2,1,0:T(8,128)} %pad_maximum_fusion.9), calls=%async_computation.1 | async-start | bytes 327680 | tf_op jit(solution)/shard_map/all_to_all | solution.py:343
  155.8 41.2 %collective-permute-start.14 = (f32[4,40,512]{2,1,0:T(8,128)}, f32[4,40,512]{2,1,0:T(8,128)}, u32[]{:S(2)}, u32[]{:S(2)}) collective-permute-start(f32[4,40,512]{2,1,0:T(8,128)} %get-tuple-element.28), channel_id=1, source_target_pairs={{0,1},{1,2},{2,3},{4,5},{5,6},{6,7},{8,9},{9,10},{10,11},{12,13},{... | collective-permute-start | bytes 983048 | tf_op jit(solution)/shard_map/ppermute | solution.py:32
  160.4 36.6 %collective-permute-start.15 = (f32[4,40,512]{2,1,0:T(8,128)}, f32[4,40,512]{2,1,0:T(8,128)}, u32[]{:S(2)}, u32[]{:S(2)}) collective-permute-start(f32[4,40,512]{2,1,0:T(8,128)} %get-tuple-element.29), channel_id=1, source_target_pairs={{1,0},{2,1},{3,2},{5,4},{6,5},{7,6},{9,8},{10,9},{11,10},{13,12},{... | collective-permute-start | bytes 983048 | tf_op jit(solution)/shard_map/ppermute | solution.py:35
  162.8 2.9 %copy-start.2 = (f32[2,312,1152]{2,1,0:T(8,128)S(1)}, f32[2,312,1152]{2,1,0:T(8,128)}, u32[]{:S(2)}) copy-start(f32[2,312,1152]{2,1,0:T(8,128)} %concatenate.30) | copy-start | bytes 8626180
  185.9 9.5 %all-to-all-start.2 = ((f32[4,38,128]{2,1,0:T(8,128)}), f32[4,38,128]{2,1,0:T(8,128)S(1)}, u32[]{:S(2)}, u32[]{:S(2)}) async-start(f32[4,38,128]{2,1,0:T(8,128)} %broadcast_in_dim.43), calls=%async_computation.2 | async-start | bytes 163840 | tf_op jit(solution)/shard_map/all_to_all | solution.py:314
  190.5 2.0 copy-start.5
  192.5 3.0 %copy-start.18 = (s32[640]{0:T(1024)S(1)}, s32[640]{0:T(1024)}, u32[]{:S(2)}) copy-start(s32[640]{0:T(1024)} %eq.123) | copy-start | bytes 7684
  192.6 3.0 %copy-start.20 = (pred[640]{0:T(1024)(128)(4,1)S(1)}, pred[640]{0:T(1024)(128)(4,1)}, u32[]{:S(2)}) copy-start(pred[640]{0:T(1024)(128)(4,1)} %and.191) | copy-start | bytes 1924
  193.9 3.1 %copy-start.12 = (f32[8,40,512]{2,1,0:T(8,128)S(1)}, f32[8,40,512]{2,1,0:T(8,128)}, u32[]{:S(2)}) copy-start(f32[8,40,512]{2,1,0:T(8,128)} %get-tuple-element.30) | copy-start | bytes 1966084
where the time goes:
time: 214 us; the launch traced here: 212 us
  starting transfers between devices  52.9 us (25%)
  Pallas kernels  49.1 us (23%)
  local copies, waits for them, and re-layouts  39 us (18%)
  other arithmetic  36.5 us (17%)
  waiting for transfers between devices  32 us (15%)
    pallas_call x2, Pallas kernels, run_power(): pl.pallas_call(kernel, out_shape=jax.ShapeDtypeStruct((n, w), jnp.float32...  27 us
    ppermute x8, waiting for transfers between devices, extended(): lax.ppermute(lax.slice_in_dim(block, 0, width, axis=dim), axis, backward)  24.3 us
    pallas_call x2, Pallas kernels, run_thermal(): pl.pallas_call(kernel, out_shape=jax.ShapeDtypeStruct((n, w), jnp.float32...  22.2 us
    ppermute x8, starting transfers between devices, extended(): lax.ppermute(lax.slice_in_dim(block, block.shape[dim] - width, None, axis...  21.4 us
    ppermute x8, starting transfers between devices, extended(): lax.ppermute(lax.slice_in_dim(block, 0, width, axis=dim), axis, backward)  19.6 us
    concatenate x4, local copies, waits for them, and re-layouts, extended(): block = jnp.concatenate([low, block, high], axis=dim)  10.8 us
    all_to_all x2, starting transfers between devices, gather_heat(): lax.all_to_all(copies, 'col', split_axis=0, concat_axis=0, tiled=True)  8.54 us
    concatenate x4, other arithmetic, extended(): block = jnp.concatenate([low, block, high], axis=dim)  8.34 us
  transfers between devices with their start and end apart: 19, of which 6 were waited for; matrix products, arithmetic and copies ran while one was open for 20% of the time, Pallas kernels for 7%

commit v1 on v0

--- a/solution.py
+++ b/solution.py
@@ -290,9 +290,8 @@
     via_g = VIA_CONDUCT * vias.astype(jnp.float32)
     load0 = demand + leakage
 
-    p0 = extended(jnp.stack([conductance, load0, via_g]), (("row", 1, R0), ("col", 2, CW)))
-    k_in, p0 = lax.optimization_barrier((jnp.stack([lateral_k, vertical_k]), p0))
-    k_ext = extended(k_in, (("col", 1, T1), ("row", 2, T0)))
+    p0 = extended(jnp.stack([conductance, load0, via_g, demand, leakage]), (("row", 1, R0), ("col", 2, CW)))
+    k_layers = extended(jnp.stack([lateral_k, vertical_k]), (("col", 1, T1),))
 
     cols_w = tile_cols + 2 * CW
     col_ok = inside_of(c_idx * tile_cols - CW, cols_w, total_cols).astype(jnp.float32)[None, :]
@@ -300,8 +299,8 @@
     rows0 = tile_rows + 2 * R0
     row_ok0 = inside_of(r_idx * tile_rows - R0, rows0, total_rows).astype(jnp.float32)[:, None]
     drop0 = run_power(None, p0, row_ok0, col_ok)
-    p1_in, layer_in, drop0 = lax.optimization_barrier((jnp.stack([demand, leakage]), layer_of, drop0))
-    p1 = extended(p1_in, (("row", 1, R1), ("col", 2, CW)))
+    k_layers, layer_in, drop0 = lax.optimization_barrier((k_layers, layer_of, drop0))
+    k_ext = extended(k_layers, (("row", 2, T0),))
     layer_ext = extended(layer_in, (("row", 0, T0),))
     hr0 = H0 * COARSE
     rs = slice(R0 - hr0, R0 + tile_rows + hr0)
@@ -351,7 +350,7 @@
     grow_f = fine_of(grow_c, cols_w)[fo:fo + rows1]
     rs1 = slice(R0 - R1, R0 - R1 + rows1)
     cond1 = p0[0][rs1] / denom_f
-    load1 = p1[0] + p1[1] * grow_f
+    load1 = p0[3][rs1] + p0[4][rs1] * grow_f
     row_ok1 = inside_of(r_idx * tile_rows - R1, rows1, total_rows).astype(jnp.float32)[:, None]
     drop1 = run_power(drop0, (cond1, load1, p0), row_ok1, col_ok, offset=(R0 - R1) // 8)
     hr1 = H1 * COARSE

time: 214 us -> 210 us (0.981)
  starting transfers between devices: 52.9 us -> 45.4 us
  other arithmetic: 36.5 us -> 30.3 us
  local copies, waits for them, and re-layouts: 39 us -> 45 us
    ppermute x8 -> x6, waiting for transfers between devices: 24.3 us -> 12.9 us  [extended(): lax.ppermute(lax.slice_in_dim(block, 0, width, axis=dim), axis, backward)]
    ppermute x8 -> x6, waiting for transfers between devices: 6.19 us -> 14.2 us  [extended(): lax.ppermute(lax.slice_in_dim(block, block.shape[dim] - width, None, axis...]
    ppermute x8 -> x6, starting transfers between devices: 19.6 us -> 12.6 us  [extended(): lax.ppermute(lax.slice_in_dim(block, 0, width, axis=dim), axis, backward)]
    all_to_all x2, waiting for transfers between devices: 1.58 us -> 6.59 us  [gather_heat(): lax.all_to_all(copies, 'col', split_axis=0, concat_axis=0, tiled=True)]
    unnamed x54 -> x48, local copies, waits for them, and re-layouts: 3.51 us -> 7.04 us
    div x1 -> x0, other arithmetic: 2.87 us -> none  [body(): cond1 = p0[0][rs1] / denom_f]
    another operation x3 -> x1, other arithmetic: 5.13 us -> 2.34 us  [body(): k_layers = extended(jnp.stack([lateral_k, vertical_k]), (('col', 1, T1),))]
    add x1, other arithmetic: 1.51 us -> 4.23 us  [body(): load1 = p0[3][rs1] + p0[4][rs1] * grow_f]
  transfers between devices with their start and end apart: 19 -> 15, of which waited for: 6 -> 6; matrix products, arithmetic and copies ran while one was open for 20% -> 20% of each run, Pallas kernels for 7% -> 7%
where the time goes in v1:
time: 210 us; the launch traced here: 208 us
  Pallas kernels  50.9 us (24%)
  starting transfers between devices  45.4 us (22%)
  local copies, waits for them, and re-layouts  45 us (21%)
  waiting for transfers between devices  33.7 us (16%)
  other arithmetic  30.3 us (14%)
    pallas_call x2, Pallas kernels, run_power(): pl.pallas_call(kernel, out_shape=jax.ShapeDtypeStruct((n, w), jnp.float32...  28.8 us
    pallas_call x2, Pallas kernels, run_thermal(): pl.pallas_call(kernel, out_shape=jax.ShapeDtypeStruct((n, w), jnp.float32...  22.1 us
    ppermute x6, starting transfers between devices, extended(): lax.ppermute(lax.slice_in_dim(block, block.shape[dim] - width, None, axis...  20.9 us
    ppermute x6, waiting for transfers between devices, extended(): lax.ppermute(lax.slice_in_dim(block, block.shape[dim] - width, None, axis...  14.2 us
    ppermute x6, waiting for transfers between devices, extended(): lax.ppermute(lax.slice_in_dim(block, 0, width, axis=dim), axis, backward)  12.9 us
    ppermute x6, starting transfers between devices, extended(): lax.ppermute(lax.slice_in_dim(block, 0, width, axis=dim), axis, backward)  12.6 us
    concatenate x3, local copies, waits for them, and re-layouts, extended(): block = jnp.concatenate([low, block, high], axis=dim)  11.1 us
    all_to_all x2, starting transfers between devices, gather_heat(): lax.all_to_all(copies, 'col', split_axis=0, concat_axis=0, tiled=True)  8.63 us
  transfers between devices with their start and end apart: 15, of which 6 were waited for; matrix products, arithmetic and copies ran while one was open for 20% of the time, Pallas kernels for 7%

profile of v1, /device:TPU:8, one launch (start us, length us, event | category | flops | bytes accessed | tf_op | source)
XLA Modules:
  0.0 208.0 jit_solution(2536526351402701416)
XLA Ops:
  0.6 2.3 %fusion.11 = (f32[2,4,32,512]{3,2,1,0:T(8,128)}, f32[2,4,32,512]{3,2,1,0:T(8,128)}) fusion(f32[1,8,32,512]{3,2,1,0:T(8,128)} %bitcast.93, f32[1,8,32,512]{3,2,1,0:T(8,128)} %bitcast.95), kind=kLoop, calls=%fused_computation.42 | loop fusion | flops 262144 | bytes 2097152 | tf_op jit(solution)/shard_map/stack | solution.py:294
  3.0 4.3 %collective-permute-start = (f32[2,4,32,512]{3,2,1,0:T(8,128)}, f32[2,4,32,512]{3,2,1,0:T(8,128)}, u32[]{:S(2)}, u32[]{:S(2)}) collective-permute-start(f32[2,4,32,512]{3,2,1,0:T(8,128)} %get-tuple-element.26), channel_id=1, source_target_pairs={{0,1},{1,2},{2,3},{4,5},{5,6},{6,7},{8,9},{9,10},{10,11},{12,13},{... | collective-permute-start | bytes 1572872 | tf_op jit(solution)/shard_map/ppermute | solution.py:32
  7.3 1.3 collective-permute-start.1
  8.9 1.1 copy-done.12
  10.5 2.0 copy-done.1
  12.5 1.9 collective-permute-start.2
  14.4 3.6 %collective-permute-start.3 = (f32[5,60,1024]{2,1,0:T(8,128)S(1)}, f32[5,60,1024]{2,1,0:T(8,128)}, u32[]{:S(2)}, u32[]{:S(2)}) collective-permute-start(f32[5,60,1024]{2,1,0:T(8,128)S(1)} %get-tuple-element.15), channel_id=1, source_target_pairs={{4,0},{8,4},{12,8},{16,12},{20,16},{24,20},{28,24},{5,1},{9,5},{13... | collective-permute-start | bytes 3686408 | tf_op jit(solution)/shard_map/ppermute | solution.py:35
  18.8 0.7 eq.123
  19.7 0.9 reshape.280.refs_4_
  20.6 0.9 reshape.279.refs_3_
  21.5 0.5 and.191
  22.1 0.6 add_select_fusion
  22.7 0.7 fusion.23.refs_4_
  23.4 0.7 fusion.19.refs_1_
  24.1 7.5 %collective-permute-done.2 = f32[5,60,1024]{2,1,0:T(8,128)} collective-permute-done((f32[5,60,1024]{2,1,0:T(8,128)S(1)}, f32[5,60,1024]{2,1,0:T(8,128)}, u32[]{:S(2)}, u32[]{:S(2)}) %collective-permute-start.2) | collective-permute-done | bytes 1228832 | tf_op jit(solution)/shard_map/ppermute | solution.py:32
  31.5 1.7 collective-permute-done.3
  33.2 3.8 %pad_maximum_fusion = f32[5,376,1024]{2,1,0:T(8,128)S(1)} fusion(f32[5,60,1024]{2,1,0:T(8,128)} %collective-permute-done.3, f32[5,256,1024]{2,1,0:T(8,128)} %copy-done.1, f32[5,60,1024]{2,1,0:T(8,128)} %collective-permute-done.2), kind=kLoop, calls=%fused_computation | loop fusion | flops 3850240 | bytes 15400960 | tf_op jit(solution)/shard_map/concatenate | solution.py:36
  37.0 3.0 %copy-done = f32[5,376,1024]{2,1,0:T(8,128)} copy-done((f32[5,376,1024]{2,1,0:T(8,128)}, f32[5,376,1024]{2,1,0:T(8,128)S(1)}, u32[]{:S(2)}) %copy-start) | copy-done | bytes 7700504
  40.4 1.1 copy.34
  41.5 1.1 copy.33
  42.6 5.3 %collective-permute-start.4 = (f32[5,376,64]{1,2,0:T(8,128)}, f32[5,376,64]{1,2,0:T(8,128)}, u32[]{:S(2)}, u32[]{:S(2)}) collective-permute-start(f32[5,376,64]{1,2,0:T(8,128)} %copy.33), channel_id=1, source_target_pairs={{0,1},{1,2},{2,3},{4,5},{5,6},{6,7},{8,9},{9,10},{10,11},{12,13},{... | collective-permute-start | bytes 1443848 | tf_op jit(solution)/shard_map/ppermute | solution.py:32
  47.9 1.3 collective-permute-start.5
  49.2 0.6 and_convert_fusion.refs_2_.refs_5_
  49.9 1.5 pad_maximum_fusion.1
  51.3 6.7 %collective-permute-done.4 = f32[5,376,64]{1,2,0:T(8,128)} collective-permute-done((f32[5,376,64]{1,2,0:T(8,128)}, f32[5,376,64]{1,2,0:T(8,128)}, u32[]{:S(2)}, u32[]{:S(2)}) %collective-permute-start.4) | collective-permute-done | bytes 481312 | tf_op jit(solution)/shard_map/ppermute | solution.py:32
  58.1 1.4 copy.35
  59.4 11.2 %collective-permute-done.5 = f32[5,376,64]{1,2,0:T(8,128)} collective-permute-done((f32[5,376,64]{1,2,0:T(8,128)}, f32[5,376,64]{1,2,0:T(8,128)}, u32[]{:S(2)}, u32[]{:S(2)}) %collective-permute-start.5) | collective-permute-done | bytes 481312 | tf_op jit(solution)/shard_map/ppermute | solution.py:35
  70.7 2.3 %copy.36 = f32[5,376,64]{2,1,0:T(8,128)} copy(f32[5,376,64]{1,2,0:T(8,128)} %collective-permute-done.5) | data formatting | bytes 962560 | tf_op jit(solution)/shard_map/ppermute | solution.py:35
  73.0 11.1 %concatenate.20.refs_0_.refs_3_ = f32[5,376,1152]{2,1,0:T(8,128)} concatenate(f32[5,376,64]{2,1,0:T(8,128)S(1)} %copy.35, f32[5,376,1024]{2,1,0:T(8,128)} %copy-done, f32[5,376,64]{2,1,0:T(8,128)} %copy.36), dimensions={2} | concatenate | bytes 17326080 | tf_op jit(solution)/shard_map/concatenate | solution.py:36
  84.1 3.9 %slice_bitcast_fusion.1 = (f32[376,1152]{1,0:T(8,128)}, f32[376,1152]{1,0:T(8,128)}) fusion(f32[5,376,1152]{2,1,0:T(8,128)} %concatenate.20.refs_0_.refs_3_), kind=kLoop, calls=%fused_computation.5 | loop fusion | bytes 6930432 | tf_op jit(solution)/shard_map/squeeze | solution.py:309
  88.0 13.6 %shard_map.86.refs_0_ = f32[376,1152]{1,0:T(8,128)} custom-call(f32[5,376,1152]{2,1,0:T(8,128)} %concatenate.20.refs_0_.refs_3_, f32[376,1]{1,0:T(8,128)} %fusion.19.refs_1_, f32[1,1152]{1,0:T(1,128)} %and_convert_fusion.refs_2_.refs_5_), custom_call_target="tpu_custom_call" | custom-call | tf_op jit(solution)/shard_map/pallas_call | solution.py:159
  101.6 2.1 collective-permute-start.7
  103.7 2.7 %collective-permute-start.6 = (s32[8,512]{1,0:T(8,128)S(1)}, s32[8,512]{1,0:T(8,128)S(1)}, u32[]{:S(2)}, u32[]{:S(2)}) collective-permute-start(s32[8,512]{1,0:T(8,128)S(1)} %get-tuple-element.33), channel_id=1, source_target_pairs={{0,4},{4,8},{8,12},{12,16},{16,20},{20,24},{24,28},{1,5},{5,9},{9,... | collective-permute-start | bytes 49160 | tf_op jit(solution)/shard_map/ppermute | solution.py:32
  106.4 1.1 fusion.46
  107.5 2.8 %collective-permute-start.9 = (f32[2,16,8,512]{3,2,1,0:T(8,128)}, f32[2,16,8,512]{3,2,1,0:T(8,128)S(1)}, u32[]{:S(2)}, u32[]{:S(2)}) collective-permute-start(f32[2,16,8,512]{3,2,1,0:T(8,128)} %get-tuple-element.20), channel_id=1, source_target_pairs={{4,0},{8,4},{12,8},{16,12},{20,16},{24,20},{28,24},{5,1},{9,5},{13... | collective-permute-start | bytes 1572872 | tf_op jit(solution)/shard_map/ppermute | solution.py:35
  110.3 2.7 %collective-permute-start.8 = (f32[2,16,8,512]{3,2,1,0:T(8,128)}, f32[2,16,8,512]{3,2,1,0:T(8,128)S(1)}, u32[]{:S(2)}, u32[]{:S(2)}) collective-permute-start(f32[2,16,8,512]{3,2,1,0:T(8,128)} %get-tuple-element.21), channel_id=1, source_target_pairs={{0,4},{4,8},{8,12},{12,16},{16,20},{20,24},{24,28},{1,5},{5,9},{9,... | collective-permute-start | bytes 1572872 | tf_op jit(solution)/shard_map/ppermute | solution.py:32
  113.0 3.4 %fusion.3 = f32[46,1024]{1,0:T(8,128)S(1)} fusion(f32[376,1152]{1,0:T(8,128)} %get-tuple-element.11, f32[376,1152]{1,0:T(8,128)} %get-tuple-element.10, f32[376,1152]{1,0:T(8,128)S(1)} %copy-done.2), kind=kLoop, calls=%fused_computation.11 | loop fusion | flops 2213888 | bytes 4710400 | tf_op jit(solution)/shard_map/reduce_sum | solution.py:55
  116.4 0.4 convolution_multiply_fusion
  116.8 0.6 broadcast_in_dim.36
  117.5 3.3 %all-to-all-start = ((f32[4,46,128]{2,1,0:T(8,128)}), f32[4,46,128]{2,1,0:T(8,128)S(1)}, u32[]{:S(2)}, u32[]{:S(2)}) async-start(f32[4,46,128]{2,1,0:T(8,128)} %broadcast_in_dim.36), calls=%async_computation | async-start | bytes 196608 | tf_op jit(solution)/shard_map/all_to_all | solution.py:313
  120.9 4.9 %all-to-all-done = f32[4,46,128]{2,1,0:T(8,128)S(1)} async-done(((f32[4,46,128]{2,1,0:T(8,128)}), f32[4,46,128]{2,1,0:T(8,128)S(1)}, u32[]{:S(2)}, u32[]{:S(2)}) %all-to-all-start) | async-done | bytes 94240 | tf_op jit(solution)/shard_map/all_to_all | solution.py:313
  125.9 1.6 bitcast_select_fusion.refs_0_
  127.7 2.1 %fusion.45 = (f32[1,16,48,512]{3,2,1,0:T(8,128)}, f32[1,16,48,512]{3,2,1,0:T(8,128)}) fusion(f32[2,16,48,512]{3,2,1,0:T(8,128)S(1)} %constant_dynamic-update-slice_fusion.3), kind=kLoop, calls=%fused_computation.107 | loop fusion | bytes 6291456 | tf_op jit(solution)/shard_map/slice | solution.py:328
  129.9 0.5 copy-done.3
  130.3 10.9 %shard_map.87 = f32[768,512]{1,0:T(8,128)} custom-call(f32[768,512]{1,0:T(8,128)} %bitcast_select_fusion.refs_0_, f32[768,512]{1,0:T(8,128)} %bitcast.86, f32[768,512]{1,0:T(8,128)} %bitcast.85, f32[768,1]{1,0:T(8,128)} %reshape.279.refs_3_), custom_call_target="tpu_custom_call" | custom-call | tf_op jit(solution)/shard_map/pallas_call | solution.py:252
  141.3 2.1 %fusion.48 = (f32[8,40,512]{2,1,0:T(8,128)}, f32[40,512]{1,0:T(8,128)S(1)}) fusion(f32[16,48,512]{2,1,0:T(8,128)} %bitcast.87, s32[8]{0:T(128)S(1)} %iota_add_fusion.3, s32[40,512]{1,0:T(8,128)S(1)} %slice.181), kind=kLoop, calls=%fused_computation.110 | loop fusion | flops 471040 | bytes 1474592 | tf_op jit(solution)/shard_map/slice | solution.py:334
  143.5 0.7 pad_maximum_fusion.4
  144.2 3.3 %all-to-all-start.1 = ((f32[4,40,144]{2,1,0:T(8,128)}), f32[4,40,144]{2,1,0:T(8,128)S(1)}, u32[]{:S(2)}, u32[]{:S(2)}) async-start(f32[4,40,144]{2,1,0:T(8,128)} %pad_maximum_fusion.4), calls=%async_computation.1 | async-start | bytes 327680 | tf_op jit(solution)/shard_map/all_to_all | solution.py:342
  147.5 2.1 fusion.47
  149.6 3.9 %collective-permute-start.10 = (f32[4,40,512]{2,1,0:T(8,128)}, f32[4,40,512]{2,1,0:T(8,128)S(1)}, u32[]{:S(2)}, u32[]{:S(2)}) collective-permute-start(f32[4,40,512]{2,1,0:T(8,128)} %get-tuple-element.22), channel_id=1, source_target_pairs={{0,1},{1,2},{2,3},{4,5},{5,6},{6,7},{8,9},{9,10},{10,11},{12,13},{... | collective-permute-start | bytes 983048 | tf_op jit(solution)/shard_map/ppermute | solution.py:32
  153.5 1.5 collective-permute-start.11
  155.9 4.2 %fusion.4 = (f32[312,1152]{1,0:T(8,128)}, f32[312,1152]{1,0:T(8,128)}) fusion(f32[320,1152]{1,0:T(8,128)S(1)} %get-tuple-element.34, f32[5,376,1152]{2,1,0:T(8,128)} %concatenate.20.refs_0_.refs_3_, f32[320,1152]{1,0:T(8,128)S(1)} %get-tuple-element.35), kind=kLoop, calls=%fused_computation.14 | loop fusion | flops 1078272 | bytes 10063872 | tf_op jit(solution)/shard_map/add | solution.py:353
  160.1 15.2 %shard_map.88 = f32[312,1152]{1,0:T(8,128)} custom-call(f32[376,1152]{1,0:T(8,128)} %shard_map.86.refs_0_, f32[312,1152]{1,0:T(8,128)} %get-tuple-element.9.refs_1_, f32[312,1152]{1,0:T(8,128)} %get-tuple-element.8.refs_2_, f32[5,376,1152]{2,1,0:T(8,128)} %concatenate.20.refs_0_.refs_3_, f32[312,1]{1,0:T(8,128)} %fusion.23.refs_4_, ...), custom_call_target="tpu_custom_call" | custom-call | tf_op jit(solution)/shard_map/pallas_call | solution.py:159
  175.4 3.5 %fusion.8 = f32[38,1024]{1,0:T(8,128)S(1)} fusion(f32[312,1152]{1,0:T(8,128)} %get-tuple-element.9.refs_1_, f32[312,1152]{1,0:T(8,128)} %get-tuple-element.8.refs_2_, f32[312,1152]{1,0:T(8,128)} %shard_map.88), kind=kLoop, calls=%fused_computation.25 | loop fusion | flops 1828864 | bytes 3891200 | tf_op jit(solution)/shard_map/reduce_sum | solution.py:55
  179.3 0.6 broadcast_in_dim.43
  180.0 5.3 %all-to-all-start.2 = ((f32[4,38,128]{2,1,0:T(8,128)}), f32[4,38,128]{2,1,0:T(8,128)}, u32[]{:S(2)}, u32[]{:S(2)}) async-start(f32[4,38,128]{2,1,0:T(8,128)} %broadcast_in_dim.43), calls=%async_computation.2 | async-start | bytes 163840 | tf_op jit(solution)/shard_map/all_to_all | solution.py:313
  185.3 2.0 fusion.44
  187.3 1.3 slice.195
  188.6 1.7 all-to-all-done.2
  190.3 0.9 copy.41
  191.3 1.4 bitcast_select_fusion.1.refs_1_
  192.7 2.2 %pad_maximum_fusion.2 = f32[16,40,512]{2,1,0:T(8,128)} fusion(f32[4,40,512]{2,1,0:T(8,128)} %collective-permute-done.11, f32[8,40,512]{2,1,0:T(8,128)S(1)} %copy-done.8, f32[4,40,512]{2,1,0:T(8,128)S(1)} %collective-permute-done.10), kind=kLoop, calls=%fused_computation.19 | loop fusion | flops 655360 | bytes 2621440 | tf_op jit(solution)/shard_map/concatenate | solution.py:36
  194.9 11.1 %shard_map.89 = f32[640,512]{1,0:T(8,128)} custom-call(f32[640,512]{1,0:T(8,128)} %bitcast.91, f32[640,512]{1,0:T(8,128)} %bitcast_select_fusion.1.refs_1_, f32[640,512]{1,0:T(8,128)} %bitcast.90, f32[640,512]{1,0:T(8,128)} %bitcast.89, f32[640,1]{1,0:T(8,128)} %reshape.280.refs_4_), custom_call_target="tpu_custom_call" | custom-call | tf_op jit(solution)/shard_map/pallas_call | solution.py:252
  206.1 1.9 slice.203
  (91 shorter events, 3.9 us)
Async XLA Ops:
  0.6 8.0 %copy-start.11 = (f32[256,1024]{1,0:T(8,128)S(1)}, f32[256,1024]{1,0:T(8,128)}, u32[]{:S(2)}) copy-start(f32[256,1024]{1,0:T(8,128)} %param.9) | copy-start | bytes 3145732
  3.0 5.7 %copy-start.6 = (f32[256,1024]{1,0:T(8,128)S(1)}, f32[256,1024]{1,0:T(8,128)}, u32[]{:S(2)}) copy-start(f32[256,1024]{1,0:T(8,128)} %param.7) | copy-start | bytes 3145732
  3.0 5.7 %copy-start.7 = (f32[256,1024]{1,0:T(8,128)S(1)}, f32[256,1024]{1,0:T(8,128)}, u32[]{:S(2)}) copy-start(f32[256,1024]{1,0:T(8,128)} %param.8) | copy-start | bytes 3145732
  3.0 46.9 %collective-permute-start = (f32[2,4,32,512]{3,2,1,0:T(8,128)}, f32[2,4,32,512]{3,2,1,0:T(8,128)}, u32[]{:S(2)}, u32[]{:S(2)}) collective-permute-start(f32[2,4,32,512]{3,2,1,0:T(8,128)} %get-tuple-element.26), channel_id=1, source_target_pairs={{0,1},{1,2},{2,3},{4,5},{5,6},{6,7},{8,9},{9,10},{10,11},{12,13},{... | collective-permute-start | bytes 1572872 | tf_op jit(solution)/shard_map/ppermute | solution.py:32
  7.3 42.5 %collective-permute-start.1 = (f32[2,4,32,512]{3,2,1,0:T(8,128)}, f32[2,4,32,512]{3,2,1,0:T(8,128)}, u32[]{:S(2)}, u32[]{:S(2)}) collective-permute-start(f32[2,4,32,512]{3,2,1,0:T(8,128)} %get-tuple-element.27), channel_id=1, source_target_pairs={{1,0},{2,1},{3,2},{5,4},{6,5},{7,6},{9,8},{10,9},{11,10},{13,12},{... | collective-permute-start | bytes 1572872 | tf_op jit(solution)/shard_map/ppermute | solution.py:35
  8.7 1.2 copy-start.12
  10.2 2.3 %copy-start.1 = (f32[5,256,1024]{2,1,0:T(8,128)}, f32[5,256,1024]{2,1,0:T(8,128)S(1)}, u32[]{:S(2)}) copy-start(f32[5,256,1024]{2,1,0:T(8,128)S(1)} %bitcast_dynamic-update-slice_fusion) | copy-start | bytes 15728644
  12.5 19.0 %collective-permute-start.2 = (f32[5,60,1024]{2,1,0:T(8,128)S(1)}, f32[5,60,1024]{2,1,0:T(8,128)}, u32[]{:S(2)}, u32[]{:S(2)}) collective-permute-start(f32[5,60,1024]{2,1,0:T(8,128)S(1)} %get-tuple-element.14), channel_id=1, source_target_pairs={{0,4},{4,8},{8,12},{12,16},{16,20},{20,24},{24,28},{1,5},{5,9},{9,... | collective-permute-start | bytes 3686408 | tf_op jit(solution)/shard_map/ppermute | solution.py:32
  14.4 18.8 %collective-permute-start.3 = (f32[5,60,1024]{2,1,0:T(8,128)S(1)}, f32[5,60,1024]{2,1,0:T(8,128)}, u32[]{:S(2)}, u32[]{:S(2)}) collective-permute-start(f32[5,60,1024]{2,1,0:T(8,128)S(1)} %get-tuple-element.15), channel_id=1, source_target_pairs={{4,0},{8,4},{12,8},{16,12},{20,16},{24,20},{28,24},{5,1},{9,5},{13... | collective-permute-start | bytes 3686408 | tf_op jit(solution)/shard_map/ppermute | solution.py:35
  22.1 94.3 %copy-start.15 = (s32[1024]{0:T(1024)}, s32[1024]{0:T(1024)S(1)}, u32[]{:S(2)}) copy-start(s32[1024]{0:T(1024)S(1)} %add_select_fusion.1) | copy-start | bytes 12292
  37.0 3.0 %copy-start = (f32[5,376,1024]{2,1,0:T(8,128)}, f32[5,376,1024]{2,1,0:T(8,128)S(1)}, u32[]{:S(2)}) copy-start(f32[5,376,1024]{2,1,0:T(8,128)S(1)} %pad_maximum_fusion) | copy-start | bytes 23101444
  40.4 9.5 %copy-start.9 = (f32[8,32,512]{2,1,0:T(8,128)S(1)}, f32[8,32,512]{2,1,0:T(8,128)}, u32[]{:S(2)}) copy-start(f32[8,32,512]{2,1,0:T(8,128)} %param.12) | copy-start | bytes 1572868
  40.4 9.5 %copy-start.10 = (f32[8,32,512]{2,1,0:T(8,128)S(1)}, f32[8,32,512]{2,1,0:T(8,128)}, u32[]{:S(2)}) copy-start(f32[8,32,512]{2,1,0:T(8,128)} %param.13) | copy-start | bytes 1572868
  42.6 15.5 %collective-permute-start.4 = (f32[5,376,64]{1,2,0:T(8,128)}, f32[5,376,64]{1,2,0:T(8,128)}, u32[]{:S(2)}, u32[]{:S(2)}) collective-permute-start(f32[5,376,64]{1,2,0:T(8,128)} %copy.33), channel_id=1, source_target_pairs={{0,1},{1,2},{2,3},{4,5},{5,6},{6,7},{8,9},{9,10},{10,11},{12,13},{... | collective-permute-start | bytes 1443848 | tf_op jit(solution)/shard_map/ppermute | solution.py:32
  47.9 22.7 %collective-permute-start.5 = (f32[5,376,64]{1,2,0:T(8,128)}, f32[5,376,64]{1,2,0:T(8,128)}, u32[]{:S(2)}, u32[]{:S(2)}) collective-permute-start(f32[5,376,64]{1,2,0:T(8,128)} %copy.34), channel_id=1, source_target_pairs={{1,0},{2,1},{3,2},{5,4},{6,5},{7,6},{9,8},{10,9},{11,10},{13,12},{... | collective-permute-start | bytes 1443848 | tf_op jit(solution)/shard_map/ppermute | solution.py:35
  88.0 13.6 %copy-start.13 = (s32[32,512]{1,0:T(8,128)S(1)}, s32[32,512]{1,0:T(8,128)}, u32[]{:S(2)}) copy-start(s32[32,512]{1,0:T(8,128)} %param.11) | copy-start | bytes 196612
  101.6 11.4 %copy-start.2 = (f32[376,1152]{1,0:T(8,128)S(1)}, f32[376,1152]{1,0:T(8,128)}, u32[]{:S(2)}) copy-start(f32[376,1152]{1,0:T(8,128)} %shard_map.86.refs_0_) | copy-start | bytes 5197828
  101.6 19.2 %collective-permute-start.7 = (s32[8,512]{1,0:T(8,128)S(1)}, s32[8,512]{1,0:T(8,128)S(1)}, u32[]{:S(2)}, u32[]{:S(2)}) collective-permute-start(s32[8,512]{1,0:T(8,128)S(1)} %get-tuple-element.32), channel_id=1, source_target_pairs={{4,0},{8,4},{12,8},{16,12},{20,16},{24,20},{28,24},{5,1},{9,5},{13... | collective-permute-start | bytes 49160 | tf_op jit(solution)/shard_map/ppermute | solution.py:35
  103.7 17.1 %collective-permute-start.6 = (s32[8,512]{1,0:T(8,128)S(1)}, s32[8,512]{1,0:T(8,128)S(1)}, u32[]{:S(2)}, u32[]{:S(2)}) collective-permute-start(s32[8,512]{1,0:T(8,128)S(1)} %get-tuple-element.33), channel_id=1, source_target_pairs={{0,4},{4,8},{8,12},{12,16},{16,20},{20,24},{24,28},{1,5},{5,9},{9,... | collective-permute-start | bytes 49160 | tf_op jit(solution)/shard_map/ppermute | solution.py:32
  107.5 20.2 %collective-permute-start.9 = (f32[2,16,8,512]{3,2,1,0:T(8,128)}, f32[2,16,8,512]{3,2,1,0:T(8,128)S(1)}, u32[]{:S(2)}, u32[]{:S(2)}) collective-permute-start(f32[2,16,8,512]{3,2,1,0:T(8,128)} %get-tuple-element.20), channel_id=1, source_target_pairs={{4,0},{8,4},{12,8},{16,12},{20,16},{24,20},{28,24},{5,1},{9,5},{13... | collective-permute-start | bytes 1572872 | tf_op jit(solution)/shard_map/ppermute | solution.py:35
  110.3 17.2 %collective-permute-start.8 = (f32[2,16,8,512]{3,2,1,0:T(8,128)}, f32[2,16,8,512]{3,2,1,0:T(8,128)S(1)}, u32[]{:S(2)}, u32[]{:S(2)}) collective-permute-start(f32[2,16,8,512]{3,2,1,0:T(8,128)} %get-tuple-element.21), channel_id=1, source_target_pairs={{0,4},{4,8},{8,12},{12,16},{16,20},{20,24},{24,28},{1,5},{5,9},{9,... | collective-permute-start | bytes 1572872 | tf_op jit(solution)/shard_map/ppermute | solution.py:32
  117.5 8.3 %all-to-all-start = ((f32[4,46,128]{2,1,0:T(8,128)}), f32[4,46,128]{2,1,0:T(8,128)S(1)}, u32[]{:S(2)}, u32[]{:S(2)}) async-start(f32[4,46,128]{2,1,0:T(8,128)} %broadcast_in_dim.36), calls=%async_computation | async-start | bytes 196608 | tf_op jit(solution)/shard_map/all_to_all | solution.py:313
  127.7 2.6 %copy-start.3 = (f32[2,16,48,512]{3,2,1,0:T(8,128)}, f32[2,16,48,512]{3,2,1,0:T(8,128)S(1)}, u32[]{:S(2)}) copy-start(f32[2,16,48,512]{3,2,1,0:T(8,128)S(1)} %constant_dynamic-update-slice_fusion.3) | copy-start | bytes 9437188
  143.4 11.6 %copy-start.14 = (s32[1152]{0:T(1024)S(1)}, s32[1152]{0:T(1024)}, u32[]{:S(2)}) copy-start(s32[1152]{0:T(1024)} %add_select_fusion) | copy-start | bytes 13828
  144.2 10.8 %all-to-all-start.1 = ((f32[4,40,144]{2,1,0:T(8,128)}), f32[4,40,144]{2,1,0:T(8,128)S(1)}, u32[]{:S(2)}, u32[]{:S(2)}) async-start(f32[4,40,144]{2,1,0:T(8,128)} %pad_maximum_fusion.4), calls=%async_computation.1 | async-start | bytes 327680 | tf_op jit(solution)/shard_map/all_to_all | solution.py:342
  149.6 43.2 %collective-permute-start.10 = (f32[4,40,512]{2,1,0:T(8,128)}, f32[4,40,512]{2,1,0:T(8,128)S(1)}, u32[]{:S(2)}, u32[]{:S(2)}) collective-permute-start(f32[4,40,512]{2,1,0:T(8,128)} %get-tuple-element.22), channel_id=1, source_target_pairs={{0,1},{1,2},{2,3},{4,5},{5,6},{6,7},{8,9},{9,10},{10,11},{12,13},{... | collective-permute-start | bytes 983048 | tf_op jit(solution)/shard_map/ppermute | solution.py:32
  153.5 39.3 %collective-permute-start.11 = (f32[4,40,512]{2,1,0:T(8,128)}, f32[4,40,512]{2,1,0:T(8,128)}, u32[]{:S(2)}, u32[]{:S(2)}) collective-permute-start(f32[4,40,512]{2,1,0:T(8,128)} %get-tuple-element.23), channel_id=1, source_target_pairs={{1,0},{2,1},{3,2},{5,4},{6,5},{7,6},{9,8},{10,9},{11,10},{13,12},{... | collective-permute-start | bytes 983048 | tf_op jit(solution)/shard_map/ppermute | solution.py:35
  175.4 3.6 %copy-start.16 = (s32[1024]{0:T(1024)S(1)}, s32[1024]{0:T(1024)}, u32[]{:S(2)}) copy-start(s32[1024]{0:T(1024)} %copy-done.15) | copy-start | bytes 12292
  175.4 9.9 %copy-start.4 = (f32[2,16,48,512]{3,2,1,0:T(8,128)S(1)}, f32[2,16,48,512]{3,2,1,0:T(8,128)}, u32[]{:S(2)}) copy-start(f32[2,16,48,512]{3,2,1,0:T(8,128)} %copy-done.3) | copy-start | bytes 9437188
  180.0 10.3 %all-to-all-start.2 = ((f32[4,38,128]{2,1,0:T(8,128)}), f32[4,38,128]{2,1,0:T(8,128)}, u32[]{:S(2)}, u32[]{:S(2)}) async-start(f32[4,38,128]{2,1,0:T(8,128)} %broadcast_in_dim.43), calls=%async_computation.2 | async-start | bytes 163840 | tf_op jit(solution)/shard_map/all_to_all | solution.py:313
  185.3 2.0 copy-start.5
  187.3 4.0 %copy-start.17 = (s32[640]{0:T(1024)S(1)}, s32[640]{0:T(1024)}, u32[]{:S(2)}) copy-start(s32[640]{0:T(1024)} %eq.123) | copy-start | bytes 7684
  187.3 4.0 %copy-start.18 = (pred[640]{0:T(1024)(128)(4,1)S(1)}, pred[640]{0:T(1024)(128)(4,1)}, u32[]{:S(2)}) copy-start(pred[640]{0:T(1024)(128)(4,1)} %and.191) | copy-start | bytes 1924
  188.6 4.1 %copy-start.8 = (f32[8,40,512]{2,1,0:T(8,128)S(1)}, f32[8,40,512]{2,1,0:T(8,128)}, u32[]{:S(2)}) copy-start(f32[8,40,512]{2,1,0:T(8,128)} %get-tuple-element.24) | copy-start | bytes 1966084
